TPU v7x, 128 devices: a whole 4x4x4 slice. The times are simulated.
128 devices in a mesh: dp: 4 (over y), seq: 8 (over z, x_hi), tensor: 4 (over x_lo, core).
Axes of the slice: x: 4 (x_hi: 2, x_lo: 2; x = x_hi * 2 + x_lo), y: 4, z: 4, core: 2. Of those that a mesh axis runs over, the one named last changes fastest.
Arguments:
- patches: bfloat16 [16384, 1664], P(('dp', 'seq')), parts along dimension 0, may hold values from -6 to 6
- image_sizes: int32 [76, 2], P('dp'), parts along dimension 0, may hold values from 0 to 32, as said below
- seg_ids: int32 [16384], P('dp'), parts along dimension 0, may hold values from 0 to 19, as said below
- pad_mask: int32 [16384], P('dp'), parts along dimension 0, may hold values from 0 to 1, as said below
- ln1_gain: float32 [1664], replicated, may hold values from 0.1 to 1.9
- qkv_weight: bfloat16 [1664, 3, 1664], P(None, None, 'tensor')
- out_weight: bfloat16 [1664, 1664], P('tensor'), may hold values from -0.15625 to 0.15625
- ln2_gain: float32 [1664], replicated, may hold values from 0.1 to 1.9
- fc1_weight: bfloat16 [1664, 8192], P(None, 'tensor'), may hold values from -0.15625 to 0.15625
- fc2_weight: bfloat16 [8192, 1664], P('tensor'), may hold values from -0.0625 to 0.0625
- proj_weight: bfloat16 [6656, 4096], P('tensor', 'seq'), may hold values from -0.078125 to 0.078125
- owners: int32 [4096, 1], P('dp'), parts along dimension 0, may hold values from 0 to 7; in each aligned block of 256 rows (0 to 255, 256 to 511, ...) at most 64 rows name the same one
Outputs:
- delivered: bfloat16 [32, 4, 64, 4096], P(('dp', 'seq'), 'tensor'), parts along dimension 0
- image_rms: float32 [76], P('dp'), parts along dimension 0
- image_peak: float32 [76], P('dp'), parts along dimension 0
There are 4 independent parts, one for each index of `dp`. A program takes and returns all parts, laid end to end along the dimension named above; an argument that names none is the same for every part. Nothing has to cross between parts.
Inputs may be any that keep to these rules, and one draw needn't show every extreme that they name: `image_sizes`: sides are even; slots are packed in slot order from token 0 without gaps; the padding after the last image is shorter than 512 tokens; some slots are 0 x 0. `seg_ids`: consistent with image_sizes: tokens of slot i in order, then 19 for the padding. `pad_mask`: 1 exactly on tokens of the images. `owners`: in each aligned block of 256 merged rows no owner is named by more than 64 rows, and one is named by exactly 64.
All inputs are finite; a program needn't handle non-finite values.
Results may differ from a plain program's by a relative error of at most 0.017.
Values may be sent and summed in bfloat16 or wider, within the bound.
No kernel may reach another device: no remote copies, remote signals or barrier semaphores. Data moves between devices by JAX's collectives and lax.ppermute only.
A program may use at most 128 MiB of HBM per device.

v0:
```python
import math

import jax
import jax.numpy as jnp
from jax import lax
from jax.sharding import PartitionSpec as P

HD = 104
PROJ = 4096
SIDE = 32


EPS = 1e-06


def shifted(value, axis, steps):
    count = lax.axis_size(axis)
    leading, last = (max(0, -steps), min(count, count - steps))
    return lax.ppermute(value, axis, [(source, source + steps) for source in range(leading, last)])


def layer_norm(values, gain):
    mean = jnp.mean(values, axis=-1, keepdims=True)
    centred = values - mean
    spread = jnp.mean(centred * centred, axis=-1, keepdims=True)
    return centred * lax.rsqrt(spread + EPS) * gain


def position_table(seg_local, image_sizes, index, width):
    heights = image_sizes[:, 0]
    widths = image_sizes[:, 1]
    areas = heights * widths
    starts = jnp.cumsum(areas) - areas
    image_ids = jnp.arange(image_sizes.shape[0], dtype=jnp.int32)
    member = (seg_local[:, None] == image_ids[None, :]).astype(jnp.int32)
    begin = jnp.sum(member * starts[None, :], axis=1)
    across = jnp.sum(member * widths[None, :], axis=1)
    offset = index - begin
    blocks = offset // 4
    inner = offset % 4
    half = jnp.maximum(across // 2, 1)
    row_pos = (2 * (blocks // half) + inner // 2).astype(jnp.float32)
    col_pos = (2 * (blocks % half) + inner % 2).astype(jnp.float32)
    quarter = width // 4
    freq = jnp.exp(jnp.arange(quarter, dtype=jnp.float32) * (-math.log(10000.0) / quarter))
    row_angle = row_pos[:, None] * freq[None, :]
    col_angle = col_pos[:, None] * freq[None, :]
    return jnp.concatenate(
        [jnp.sin(row_angle), jnp.cos(row_angle), jnp.sin(col_angle), jnp.cos(col_angle)], axis=1
    )


def key_labels(block_start, tok_rows, seg_ids, pad_mask):
    total = seg_ids.shape[0]
    index = block_start + jnp.arange(tok_rows, dtype=jnp.int32)
    inside = (index >= 0) & (index < total)
    clamped = jnp.clip(block_start, 0, total - tok_rows)
    seg_part = lax.dynamic_slice_in_dim(seg_ids, clamped, tok_rows)
    mask_part = lax.dynamic_slice_in_dim(pad_mask, clamped, tok_rows)
    return (jnp.where(inside, seg_part, -1), inside & (mask_part == 1))


def local(
    patches,
    image_sizes,
    seg_ids,
    pad_mask,
    ln1_gain,
    qkv_weight,
    out_weight,
    ln2_gain,
    fc1_weight,
    fc2_weight,
    proj_weight,
    owners,
):
    tok_rows, width = patches.shape
    seq_count = lax.axis_size("seq")
    tensor_count = lax.axis_size("tensor")
    seq_rank = lax.axis_index("seq")
    tensor_rank = lax.axis_index("tensor")
    first = seq_rank * tok_rows
    index = first + jnp.arange(tok_rows, dtype=jnp.int32)
    seg_local = lax.dynamic_slice_in_dim(seg_ids, first, tok_rows)
    valid_local = lax.dynamic_slice_in_dim(pad_mask, first, tok_rows).astype(jnp.float32)
    x0 = (
        patches.astype(jnp.float32)
        + position_table(seg_local, image_sizes, index, width) * valid_local[:, None]
    )
    h1 = layer_norm(x0, ln1_gain).astype(jnp.bfloat16)
    local_width = qkv_weight.shape[2]
    heads = local_width // HD
    qkv = jnp.dot(
        h1, qkv_weight.reshape(width, 3 * local_width), preferred_element_type=jnp.float32
    )
    qkv = qkv.astype(jnp.bfloat16).reshape(tok_rows, 3, local_width)
    queries = qkv[:, 0].reshape(tok_rows, heads, HD)
    pairs = qkv[:, 1:]
    reach = min((SIDE * SIDE + tok_rows - 2) // tok_rows, seq_count - 1)
    blocks = [pairs]
    block_starts = [first]
    for step in range(1, reach + 1):
        blocks.append(shifted(pairs, "seq", step))
        block_starts.append(first - step * tok_rows)
        blocks.append(shifted(pairs, "seq", -step))
        block_starts.append(first + step * tok_rows)
    labels = [key_labels(start, tok_rows, seg_ids, pad_mask) for start in block_starts]
    key_seg = jnp.concatenate([item[0] for item in labels])
    key_ok = jnp.concatenate([item[1] for item in labels])
    gathered_pairs = jnp.concatenate(blocks, axis=0)
    keys = gathered_pairs[:, 0].reshape(-1, heads, HD)
    values = gathered_pairs[:, 1].reshape(-1, heads, HD)
    allowed = ((seg_local[:, None] == key_seg[None, :]) & key_ok[None, :])[None, :, :]
    scores = jnp.einsum("qhe,khe->hqk", queries, keys, preferred_element_type=jnp.float32) * HD ** (
        -0.5
    )
    best = jnp.max(jnp.where(allowed, scores, -1e30), axis=2, keepdims=True)
    weights = jnp.where(allowed, jnp.exp(scores - best), 0.0)
    total = jnp.sum(weights, axis=2)
    mixed = jnp.einsum(
        "hqk,khe->qhe", weights.astype(jnp.bfloat16), values, preferred_element_type=jnp.float32
    )
    attended = (
        (mixed / jnp.maximum(total, 1.0).T[:, :, None])
        .astype(jnp.bfloat16)
        .reshape(tok_rows, local_width)
    )
    partial_attn = jnp.dot(attended, out_weight, preferred_element_type=jnp.float32)
    groups = tok_rows // 4

    def pick_rows(array):
        return lax.dynamic_index_in_dim(
            array.reshape(groups, 4, -1), tensor_rank, 1, keepdims=False
        )

    valid_rows = pick_rows(valid_local[:, None])
    x1 = x0 + lax.psum(partial_attn.astype(jnp.bfloat16), "tensor").astype(jnp.float32)
    h2 = layer_norm(x1, ln2_gain).astype(jnp.bfloat16)
    hidden = jax.nn.gelu(
        jnp.dot(h2, fc1_weight, preferred_element_type=jnp.float32), approximate=False
    ).astype(jnp.bfloat16)
    mlp_full = lax.psum(
        jnp.dot(hidden, fc2_weight, preferred_element_type=jnp.float32)
        .reshape(groups, 4, width)
        .astype(jnp.bfloat16),
        "tensor",
    ).astype(jnp.float32)
    mlp_part = pick_rows(mlp_full)
    x1_rows = pick_rows(x1)
    own_quarter = ((x1_rows + mlp_part) * valid_rows).astype(jnp.bfloat16)
    all_merged = lax.all_gather(own_quarter, "seq", axis=0, tiled=True)
    quarter_rows = all_merged.shape[0] // tensor_count
    proj_part = lax.psum_scatter(
        jnp.dot(all_merged, proj_weight, preferred_element_type=jnp.float32).astype(jnp.bfloat16),
        "tensor",
        scatter_dimension=0,
        tiled=True,
    ).astype(jnp.float32)
    row_begin = tensor_rank * quarter_rows
    merged_seg = lax.dynamic_slice_in_dim(seg_ids.reshape(-1, 4)[:, 0], row_begin, quarter_rows)
    merged_valid = lax.dynamic_slice_in_dim(pad_mask.reshape(-1, 4)[:, 0], row_begin, quarter_rows)
    image_ids = jnp.arange(image_sizes.shape[0], dtype=jnp.int32)
    member = ((merged_seg[:, None] == image_ids[None, :]) & (merged_valid[:, None] == 1)).astype(
        jnp.float32
    )
    row_squares = jnp.sum(proj_part * proj_part, axis=1)
    row_peak = jnp.max(jnp.abs(proj_part), axis=1)
    local_sums = jnp.dot(row_squares, member, precision=lax.Precision.HIGHEST)
    local_peaks = jnp.max(jnp.where(member > 0, row_peak[:, None], 0.0), axis=0)
    sums = lax.psum(local_sums, ("seq", "tensor"))
    image_peak = lax.pmax(local_peaks, ("seq", "tensor"))
    counts = (image_sizes[:, 0] * image_sizes[:, 1] // 4).astype(jnp.float32)
    image_rms = jnp.sqrt(sums / (PROJ * jnp.maximum(counts, 1.0)))
    emb = proj_part.astype(jnp.bfloat16)
    capacity = 2 * quarter_rows // seq_count
    owner_rows = lax.dynamic_slice_in_dim(owners[:, 0], row_begin, quarter_rows)
    onehot = (owner_rows[:, None] == jnp.arange(seq_count, dtype=jnp.int32)[None, :]).astype(
        jnp.int32
    )
    rank = jnp.cumsum(onehot, axis=0) - onehot
    slot = jnp.sum(onehot * rank, axis=1)
    target = owner_rows * capacity + slot
    place = (jnp.arange(seq_count * capacity, dtype=jnp.int32)[:, None] == target[None, :]).astype(
        jnp.bfloat16
    )
    buffer = jnp.dot(place, emb, preferred_element_type=jnp.float32).astype(jnp.bfloat16)
    buffer = buffer.reshape(seq_count, capacity, emb.shape[1])
    arrived = lax.all_to_all(buffer, "seq", split_axis=0, concat_axis=2, tiled=True)
    delivered = arrived.reshape(1, 1, capacity, arrived.shape[2])
    return (delivered, image_rms, image_peak)


def solution(mesh):
    in_specs = (
        P(("dp", "seq"), None),
        P("dp", None),
        P("dp"),
        P("dp"),
        P(),
        P(None, None, "tensor"),
        P("tensor", None),
        P(),
        P(None, "tensor"),
        P("tensor", None),
        P("tensor", "seq"),
        P("dp", None),
    )
    out_specs = (P(("dp", "seq"), "tensor", None, None), P("dp"), P("dp"))
    return jax.shard_map(local, mesh=mesh, in_specs=in_specs, out_specs=out_specs, check_vma=False)
```

profile of v0, /device:TPU:1, one launch (start us, length us, event | category | flops | bytes accessed | tf_op | source)
XLA Modules:
  0.0 497.2 jit_solution(1094850987392276432)
XLA Ops:
  13.2 8.9 %multiply_cosine_fusion = (f32[512,416]{1,0:T(8,128)}, f32[512,416]{1,0:T(8,128)}, f32[512,416]{1,0:T(8,128)}, f32[512,416]{1,0:T(8,128)}) fusion(f32[512]{0:T(512)S(1)} %get-tuple-element.21, f32[416]{0:T(512)S(1)} %multiply_exponential_fusion, f32[512]{0:T(512)S(1)} %get-tuple-element.22), kind=kLoop, calls=%fused_computation.77 | loop fusion | flops 425984 | bytes 3413632 | tf_op jit(solution)/shard_map/cos | solution.py:49
  22.1 5.0 %concatenate.12 = f32[512,1664]{1,0:T(8,128)} concatenate(f32[512,416]{1,0:T(8,128)} %get-tuple-element.25, f32[512,416]{1,0:T(8,128)} %get-tuple-element.26, f32[512,416]{1,0:T(8,128)} %get-tuple-element.20, f32[512,416]{1,0:T(8,128)} %get-tuple-element.19), dimensions={1} | concatenate | bytes 6815744 | tf_op jit(solution)/shard_map/concatenate | solution.py:48
  27.1 2.7 fusion.152
  31.4 2.8 convolution_convert_fusion.2
  36.7 6.4 %collective-permute-start = (bf16[512,2,416]{0,2,1:T(8,128)(2,1)}, bf16[512,2,416]{0,2,1:T(8,128)(2,1)}, u32[]{:S(2)}, u32[]{:S(2)}) collective-permute-start(bf16[512,2,416]{0,2,1:T(8,128)(2,1)} %get-tuple-element.11), channel_id=1, source_target_pairs={{0,4},{4,8},{8,12},{12,16},{16,20},{20,24},{24,28},{1,5},{5,9},{9,... | collective-permute-start | bytes 2555912 | tf_op jit(solution)/shard_map/ppermute | solution.py:19
  44.3 5.3 %collective-permute-start.2 = (bf16[512,2,416]{0,2,1:T(8,128)(2,1)}, bf16[512,2,416]{0,2,1:T(8,128)(2,1)}, u32[]{:S(2)}, u32[]{:S(2)}) collective-permute-start(bf16[512,2,416]{0,2,1:T(8,128)(2,1)} %get-tuple-element.11), channel_id=1, source_target_pairs={{0,8},{4,12},{8,16},{12,20},{16,24},{20,28},{1,9},{5,13},{9,17},{1... | collective-permute-start | bytes 2555912 | tf_op jit(solution)/shard_map/ppermute | solution.py:19
  52.2 1.8 slice.45
  54.0 2.0 compare_and_fusion
  56.0 4.1 collective-permute-done
  60.1 2.2 constant_dynamic-update-slice_fusion.3
  62.3 18.4 %collective-permute-done.1 = bf16[512,2,416]{0,2,1:T(8,128)(2,1)} collective-permute-done((bf16[512,2,416]{0,2,1:T(8,128)(2,1)}, bf16[512,2,416]{0,2,1:T(8,128)(2,1)}, u32[]{:S(2)}, u32[]{:S(2)}) %collective-permute-start.1) | collective-permute-done | bytes 852000 | tf_op jit(solution)/shard_map/ppermute | solution.py:19
  80.6 2.2 constant_dynamic-update-slice_fusion.2
  82.8 2.3 constant_dynamic-update-slice_fusion.1
  85.1 2.2 constant_dynamic-update-slice_fusion
  87.2 4.5 fusion.154
  91.7 15.5 %fusion.156 = (f32[4,512]{1,0:T(4,128)S(1)}, bf16[4,512,2560]{2,1,0:T(8,128)(2,1)}) fusion(pred[512,2560]{1,0:T(8,128)(4,1)} %compare_and_fusion, bf16[512,4,104]{0,2,1:T(8,128)(2,1)} %bitcast.73, bf16[2560,4,104]{0,2,1:T(8,128)(2,1)} %bitcast.67), kind=kOutput, calls=%fused_computation.250 | convolution fusion | flops 2217740800 | bytes 14360576 | tf_op jit(solution)/shard_map/sub | solution.py:118
  107.2 8.0 %fusion.69 = bf16[512,4,104]{0,2,1:T(8,128)(2,1)S(1)} fusion(bf16[2560,4,104]{0,2,1:T(8,128)(2,1)} %bitcast.66, bf16[4,512,2560]{2,1,0:T(8,128)(2,1)} %get-tuple-element.30, f32[512,4]{0,1:T(4,128)S(1)} %maximum_bitcast_fusion), kind=kOutput, calls=%fused_computation.85 | convolution fusion | flops 1090945024 | bytes 13049856 | tf_op jit(solution)/shard_map/hqk,khe->qhe/dot_general | solution.py:120
  115.3 2.3 convolution_convert_fusion
  117.9 57.8 %all-reduce.3.cloned.1.call-done = bf16[512,1664]{1,0:T(8,128)(2,1)} async-done(((bf16[512,1664]{1,0:T(8,128)(2,1)}), bf16[512,1664]{1,0:T(8,128)(2,1)}) %all-reduce.3.cloned.1.call-update) | async-done | bytes 1703952 | tf_op jit(solution)/shard_map/psum | solution.py:137
  175.7 3.3 fusion.153
  179.0 1.7 copy-done.2
  181.2 20.8 %convolution_convert_fusion.1 = bf16[512,1664]{1,0:T(8,128)(2,1)S(1)} fusion(bf16[2048,1664]{1,0:T(8,128)(2,1)} %param.21, bf16[1664,2048]{1,0:T(8,128)(2,1)} %param.20, f32[512,1664]{1,0:T(8,128)} %copy-done.2, f32[1664]{0:T(1024)S(1)} %copy-done.11, f32[512]{0:T(512)S(1)} %add_rsqrt_fusion, f32[512]{0:T(512)S(1)} %broadcast_multiply_fusion), kind=kOutput, calls=%fused_computation.37 | convolution fusion | flops 7051739136 | bytes 18754048 | tf_op jit(solution)/shard_map/dot_general | solution.py:143
  203.8 5.0 %reshape.287 = f32[128,4,1664]{2,1,0:T(4,128)} reshape(f32[512,1664]{1,0:T(8,128)} %copy-done.2) | data formatting | bytes 6815744 | tf_op jit(solution)/shard_map/reshape | solution.py:133
  208.8 46.5 %all-reduce.5.cloned.1.call-done = bf16[128,4,1664]{2,1,0:T(4,128)(2,1)} async-done(((bf16[128,4,1664]{2,1,0:T(4,128)(2,1)}), bf16[128,4,1664]{2,1,0:T(4,128)(2,1)}) %all-reduce.5.cloned.1.call-update) | async-done | bytes 1703952 | tf_op jit(solution)/shard_map/psum | solution.py:142
  255.3 3.8 fusion.72
  260.1 64.6 %all-gather.2.cloned.1.call-done = bf16[1024,1664]{1,0:T(8,128)(2,1)} async-done(((bf16[128,1664]{1,0:T(8,128)(2,1)}), bf16[1024,1664]{1,0:T(8,128)(2,1)}) %all-gather.2.cloned.1.call-update) | async-done | bytes 3407888 | tf_op jit(solution)/shard_map/all_gather | solution.py:151
  324.6 5.0 %convolution_convert_fusion.3 = bf16[1024,512]{1,0:T(8,128)(2,1)} fusion(bf16[1024,1664]{1,0:T(8,128)(2,1)} %all-gather.2.cloned.1.call-done, bf16[1664,512]{1,0:T(8,128)(2,1)S(1)} %copy-done), kind=kOutput, calls=%fused_computation.81 | convolution fusion | flops 1745354752 | bytes 6160384 | tf_op jit(solution)/shard_map/dot_general | solution.py:154
  332.6 16.4 %reduce-scatter.2.cloned.1.call-done = bf16[256,512]{1,0:T(8,128)(2,1)} async-done(((bf16[1024,512]{1,0:T(8,128)(2,1)}), bf16[256,512]{1,0:T(8,128)(2,1)}) %reduce-scatter.2.cloned.1.call-update) | async-done | bytes 262160 | tf_op jit(solution)/shard_map/reduce_scatter | solution.py:153
  349.1 2.1 convolution_convert_fusion.4
  351.1 6.2 %all-to-all-start = ((bf16[8,64,512]{2,1,0:T(8,128)(2,1)}), bf16[8,64,512]{2,1,0:T(8,128)(2,1)S(1)}, u32[]{:S(2)}, u32[]{:S(2)}) async-start(bf16[8,64,512]{2,1,0:T(8,128)(2,1)} %bitcast.14), calls=%async_computation.1 | async-start | bytes 1048576 | tf_op jit(solution)/shard_map/all_to_all | solution.py:188
  358.7 62.9 %psum.23 = f32[19]{0:T(128)S(1)} all-reduce(f32[19]{0:T(128)S(1)} %convolution_bitcast_fusion), channel_id=1, replica_groups=mesh['dp'=4,'seq'=8,'tensor'=4] {'seq','tensor'}, use_global_device_ids=true, to_apply=%region_16.17 | all-reduce | flops 19 | bytes 152 | tf_op jit(solution)/shard_map/psum | solution.py:170
  421.6 67.2 %pmax.7 = f32[19]{0:T(128)} all-reduce(f32[19]{0:T(128)S(1)} %select_reduce_fusion.3), channel_id=1, replica_groups=mesh['dp'=4,'seq'=8,'tensor'=4] {'seq','tensor'}, use_global_device_ids=true, to_apply=%region_19.20 | all-reduce | flops 19 | bytes 152 | tf_op jit(solution)/shard_map/pmax | solution.py:171
  (87 shorter events, 23.5 us)
Async XLA Ops:
  7.2 317.5 %copy-start = (bf16[1664,512]{1,0:T(8,128)(2,1)S(1)}, bf16[1664,512]{1,0:T(8,128)(2,1)}, u32[]{:S(2)}) copy-start(bf16[1664,512]{1,0:T(8,128)(2,1)} %param.22) | copy-start | bytes 5111812
  7.2 168.5 %all-reduce.3.cloned.1.call-start = ((), (), s32[]{:S(2)}) async-start(), calls=%async_computation.2 | async-start | bytes 3407872 | tf_op jit(solution)/shard_map/psum | solution.py:137
  22.1 5.0 %copy-start.3 = (bf16[512,1664]{1,0:T(8,128)(2,1)S(1)}, bf16[512,1664]{1,0:T(8,128)(2,1)}, u32[]{:S(2)}) copy-start(bf16[512,1664]{1,0:T(8,128)(2,1)} %param.12) | copy-start | bytes 5111812
  27.1 3.0 copy-start.1
  27.1 4.2 copy-start.8
  27.1 4.2 copy-start.10
  31.4 19.8 %copy-start.6 = (s32[4096]{0:T(1024)S(1)}, s32[4096]{0:T(1024)}, u32[]{:S(2)}) copy-start(s32[4096]{0:T(1024)} %param.15) | copy-start | bytes 49156
  34.2 1.1 copy-start.4
  36.7 23.4 %collective-permute-start = (bf16[512,2,416]{0,2,1:T(8,128)(2,1)}, bf16[512,2,416]{0,2,1:T(8,128)(2,1)}, u32[]{:S(2)}, u32[]{:S(2)}) collective-permute-start(bf16[512,2,416]{0,2,1:T(8,128)(2,1)} %get-tuple-element.11), channel_id=1, source_target_pairs={{0,4},{4,8},{8,12},{12,16},{16,20},{20,24},{24,28},{1,5},{5,9},{9,... | collective-permute-start | bytes 2555912 | tf_op jit(solution)/shard_map/ppermute | solution.py:19
  43.1 37.6 %collective-permute-start.1 = (bf16[512,2,416]{0,2,1:T(8,128)(2,1)}, bf16[512,2,416]{0,2,1:T(8,128)(2,1)}, u32[]{:S(2)}, u32[]{:S(2)}) collective-permute-start(bf16[512,2,416]{0,2,1:T(8,128)(2,1)} %get-tuple-element.11), channel_id=1, source_target_pairs={{4,0},{8,4},{12,8},{16,12},{20,16},{24,20},{28,24},{5,1},{9,5},{13... | collective-permute-start | bytes 2555912 | tf_op jit(solution)/shard_map/ppermute | solution.py:19
  44.3 38.5 %collective-permute-start.2 = (bf16[512,2,416]{0,2,1:T(8,128)(2,1)}, bf16[512,2,416]{0,2,1:T(8,128)(2,1)}, u32[]{:S(2)}, u32[]{:S(2)}) collective-permute-start(bf16[512,2,416]{0,2,1:T(8,128)(2,1)} %get-tuple-element.11), channel_id=1, source_target_pairs={{0,8},{4,12},{8,16},{12,20},{16,24},{20,28},{1,9},{5,13},{9,17},{1... | collective-permute-start | bytes 2555912 | tf_op jit(solution)/shard_map/ppermute | solution.py:19
  49.7 35.4 %collective-permute-start.3 = (bf16[512,2,416]{0,2,1:T(8,128)(2,1)}, bf16[512,2,416]{0,2,1:T(8,128)(2,1)}, u32[]{:S(2)}, u32[]{:S(2)}) collective-permute-start(bf16[512,2,416]{0,2,1:T(8,128)(2,1)} %get-tuple-element.11), channel_id=1, source_target_pairs={{8,0},{12,4},{16,8},{20,12},{24,16},{28,20},{9,1},{13,5},{17,9},{2... | collective-permute-start | bytes 2555912 | tf_op jit(solution)/shard_map/ppermute | solution.py:19
  107.2 8.0 %copy-start.9 = (bf16[416,1664]{1,0:T(8,128)(2,1)S(1)}, bf16[416,1664]{1,0:T(8,128)(2,1)}, u32[]{:S(2)}) copy-start(bf16[416,1664]{1,0:T(8,128)(2,1)} %param.18) | copy-start | bytes 4153348
  117.6 63.6 %copy-start.11 = (f32[1664]{0:T(1024)S(1)}, f32[1664]{0:T(1024)}, u32[]{:S(2)}) copy-start(f32[1664]{0:T(1024)} %param.19) | copy-start | bytes 19972
  117.6 137.7 %all-reduce.5.cloned.1.call-start = ((), (), s32[]{:S(2)}) async-start(), calls=%async_computation.3 | async-start | bytes 3407872 | tf_op jit(solution)/shard_map/psum | solution.py:142
  179.0 1.7 copy-start.2
  203.5 121.2 %all-gather.2.cloned.1.call-start = ((), (), s32[]{:S(2)}) async-start(), calls=%async_computation.4 | async-start | bytes 3833856 | tf_op jit(solution)/shard_map/all_gather | solution.py:151
  260.0 69.7 %copy-start.5 = (s32[4096]{0:T(1024)S(1)}, s32[4096]{0:T(1024)}, u32[]{:S(2)}) copy-start(s32[4096]{0:T(1024)} %param.14) | copy-start | bytes 49156
  260.0 89.1 %reduce-scatter.2.cloned.1.call-start = ((), (), s32[]{:S(2)}) async-start(), calls=%async_computation.5 | async-start | bytes 1310720 | tf_op jit(solution)/shard_map/reduce_scatter | solution.py:153
  329.6 159.2 %copy-start.7 = (s32[19,2]{0,1:T(2,128)S(1)}, s32[19,2]{0,1:T(2,128)}, u32[]{:S(2)}) copy-start(s32[19,2]{0,1:T(2,128)} %param.13) | copy-start | bytes 460
  351.1 138.2 %all-to-all-start = ((bf16[8,64,512]{2,1,0:T(8,128)(2,1)}), bf16[8,64,512]{2,1,0:T(8,128)(2,1)S(1)}, u32[]{:S(2)}, u32[]{:S(2)}) async-start(bf16[8,64,512]{2,1,0:T(8,128)(2,1)} %bitcast.14), calls=%async_computation.1 | async-start | bytes 1048576 | tf_op jit(solution)/shard_map/all_to_all | solution.py:188
Sparse Core Ops, SparseCore 0:
  117.7 57.9 all-reduce.2
  203.6 51.6 all-reduce.4
  260.1 64.4 all-gather.1
  329.8 19.2 reduce-scatter.1
where the time goes:
time: 498 us; the launch traced here: 497 us
  waiting for transfers between devices  208 us (42%)
  blocking collectives  130 us (26%)
  matrix products  56.6 us (11%)
  local copies, waits for them, and re-layouts  36.2 us (7%)
  other arithmetic  31.5 us (6%)
  starting transfers between devices  21.1 us (4%)
  between operations  14 us (3%)
    pmax x1, blocking collectives, local(): image_peak = lax.pmax(local_peaks, ('seq', 'tensor'))  67.2 us
    all_gather x1, waiting for transfers between devices, local(): all_merged = lax.all_gather(own_quarter, 'seq', axis=0, tiled=True)  64.6 us
    psum x1, blocking collectives, local(): sums = lax.psum(local_sums, ('seq', 'tensor'))  62.9 us
    psum x1, waiting for transfers between devices, local(): lax.psum(partial_attn.astype(jnp.bfloat16), 'tensor').astype(jnp.float32)  57.8 us
    psum x1, waiting for transfers between devices, local(): lax.psum(jnp.dot(hidden, fc2_weight, preferred_element_type=jnp.float32)....  46.5 us
    ppermute x4, waiting for transfers between devices, shifted(): lax.ppermute(value, axis, [(source, source + steps) for source in range(l...  22.4 us
    dot_general x1, matrix products, local(): jnp.dot(hidden, fc2_weight, preferred_element_type=jnp.float32)  20.8 us
    reduce_scatter x1, waiting for transfers between devices, local(): lax.psum_scatter(jnp.dot(all_merged, proj_weight, preferred_element_type=...  16.4 us
  transfers between devices with their start and end apart: 9, of which 6 were waited for; matrix products, arithmetic and copies ran while one was open for 4% of the time, Pallas kernels for 0%

commit v1 on v0

--- a/solution.py
+++ b/solution.py
@@ -39,14 +39,14 @@
     blocks = offset // 4
     inner = offset % 4
     half = jnp.maximum(across // 2, 1)
-    row_pos = (2 * (blocks // half) + inner // 2).astype(jnp.float32)
-    col_pos = (2 * (blocks % half) + inner % 2).astype(jnp.float32)
+    row_pos = jnp.clip(2 * (blocks // half) + inner // 2, 0, SIDE - 1)
+    col_pos = jnp.clip(2 * (blocks % half) + inner % 2, 0, SIDE - 1)
     quarter = width // 4
     freq = jnp.exp(jnp.arange(quarter, dtype=jnp.float32) * (-math.log(10000.0) / quarter))
-    row_angle = row_pos[:, None] * freq[None, :]
-    col_angle = col_pos[:, None] * freq[None, :]
+    angle = jnp.arange(SIDE, dtype=jnp.float32)[:, None] * freq[None, :]
+    table = jnp.concatenate([jnp.sin(angle), jnp.cos(angle)], axis=1)
     return jnp.concatenate(
-        [jnp.sin(row_angle), jnp.cos(row_angle), jnp.sin(col_angle), jnp.cos(col_angle)], axis=1
+        [jnp.take(table, row_pos, axis=0), jnp.take(table, col_pos, axis=0)], axis=1
     )
 
 
@@ -139,13 +139,13 @@
     hidden = jax.nn.gelu(
         jnp.dot(h2, fc1_weight, preferred_element_type=jnp.float32), approximate=False
     ).astype(jnp.bfloat16)
-    mlp_full = lax.psum(
-        jnp.dot(hidden, fc2_weight, preferred_element_type=jnp.float32)
-        .reshape(groups, 4, width)
-        .astype(jnp.bfloat16),
+    mlp_out = jnp.dot(hidden, fc2_weight, preferred_element_type=jnp.float32)
+    mlp_part = lax.psum_scatter(
+        mlp_out.reshape(groups, 4, width).transpose(1, 0, 2).astype(jnp.bfloat16),
         "tensor",
-    ).astype(jnp.float32)
-    mlp_part = pick_rows(mlp_full)
+        scatter_dimension=0,
+        tiled=True,
+    ).reshape(groups, width).astype(jnp.float32)
     x1_rows = pick_rows(x1)
     own_quarter = ((x1_rows + mlp_part) * valid_rows).astype(jnp.bfloat16)
     all_merged = lax.all_gather(own_quarter, "seq", axis=0, tiled=True)
@@ -167,8 +167,12 @@
     row_peak = jnp.max(jnp.abs(proj_part), axis=1)
     local_sums = jnp.dot(row_squares, member, precision=lax.Precision.HIGHEST)
     local_peaks = jnp.max(jnp.where(member > 0, row_peak[:, None], 0.0), axis=0)
-    sums = lax.psum(local_sums, ("seq", "tensor"))
-    image_peak = lax.pmax(local_peaks, ("seq", "tensor"))
+    dp_count = lax.axis_size("dp")
+    dp_rank = lax.axis_index("dp")
+    slots = jnp.arange(dp_count, dtype=jnp.int32)[:, None] == dp_rank
+    everyone = ("dp", "seq", "tensor")
+    sums = lax.psum(jnp.where(slots, local_sums[None, :], 0.0), everyone)[dp_rank]
+    image_peak = lax.pmax(jnp.where(slots, local_peaks[None, :], 0.0), everyone)[dp_rank]
     counts = (image_sizes[:, 0] * image_sizes[:, 1] // 4).astype(jnp.float32)
     image_rms = jnp.sqrt(sums / (PROJ * jnp.maximum(counts, 1.0)))
     emb = proj_part.astype(jnp.bfloat16)

time: 498 us -> 476 us (0.956); the launches traced: 497 us -> 469 us
  waiting for transfers between devices: 208 us -> 177 us
  local copies, waits for them, and re-layouts: 36.2 us -> 44.8 us
  other arithmetic: 31.5 us -> 24.9 us
    psum x1 -> x0, waiting for transfers between devices: 46.5 us -> none  [local(): lax.psum(jnp.dot(hidden, fc2_weight, preferred_element_type=jnp.float32)....]
    reduce_scatter x0 -> x1, waiting for transfers between devices: none -> 17.8 us  [local(): lax.psum_scatter(mlp_out.reshape(groups, 4, width).transpose(1, 0, 2).ast...]
    cos x1 -> x0, other arithmetic: 8.86 us -> none  [position_table(): jnp.cos(col_angle)]
    gather x0 -> x2, local copies, waits for them, and re-layouts: none -> 5.34 us  [the longest x1 2.68 us: position_table(): jnp.take(table, col_pos, axis=0)]
    concatenate x1 -> x0, local copies, waits for them, and re-layouts: 5.02 us -> none  [position_table(): jnp.concatenate([jnp.sin(row_angle), jnp.cos(row_angle), jnp.sin(col_angl...]
    unnamed x31 -> x35, local copies, waits for them, and re-layouts: 11 us -> 13.1 us
  transfers between devices with their start and end apart: 9 -> 9, of which waited for: 6 -> 6; matrix products, arithmetic and copies ran while one was open for 4% -> 6% of each run, Pallas kernels for 0% -> 0%
where the time goes in v1:
time: 476 us; the launch traced here: 469 us
  waiting for transfers between devices  177 us (37%)
  blocking collectives  129 us (27%)
  matrix products  57.7 us (12%)
  local copies, waits for them, and re-layouts  44.8 us (9%)
  other arithmetic  24.9 us (5%)
  starting transfers between devices  21.1 us (4%)
  between operations  14.5 us (3%)
    psum x1, blocking collectives, local(): lax.psum(jnp.where(slots, local_sums[None, :], 0.0), everyone)[dp_rank]  66.3 us
    all_gather x1, waiting for transfers between devices, local(): all_merged = lax.all_gather(own_quarter, 'seq', axis=0, tiled=True)  65.5 us
    pmax x1, blocking collectives, local(): lax.pmax(jnp.where(slots, local_peaks[None, :], 0.0), everyone)[dp_rank]  62.6 us
    psum x1, waiting for transfers between devices, local(): lax.psum(partial_attn.astype(jnp.bfloat16), 'tensor').astype(jnp.float32)  57.9 us
    dot_general x1, matrix products, local(): mlp_out = jnp.dot(hidden, fc2_weight, preferred_element_type=jnp.float32)  22 us
    ppermute x4, waiting for transfers between devices, shifted(): lax.ppermute(value, axis, [(source, source + steps) for source in range(l...  19.3 us
    reduce_scatter x1, waiting for transfers between devices, local(): lax.psum_scatter(mlp_out.reshape(groups, 4, width).transpose(1, 0, 2).ast...  17.8 us
    reduce_scatter x1, waiting for transfers between devices, local(): lax.psum_scatter(jnp.dot(all_merged, proj_weight, preferred_element_type=...  16.4 us
  transfers between devices with their start and end apart: 9, of which 6 were waited for; matrix products, arithmetic and copies ran while one was open for 6% of the time, Pallas kernels for 0%

profile of v1, /device:TPU:1, one launch (start us, length us, event | category | flops | bytes accessed | tf_op | source)
XLA Modules:
  0.0 469.1 jit_solution(10973895454587112052)
XLA Ops:
  15.8 2.7 gather_fusion.1
  18.5 2.7 gather_fusion
  21.1 1.8 broadcast_select_fusion
  26.5 2.9 convolution_convert_fusion.2
  31.9 6.4 %collective-permute-start = (bf16[512,2,416]{0,2,1:T(8,128)(2,1)}, bf16[512,2,416]{0,2,1:T(8,128)(2,1)}, u32[]{:S(2)}, u32[]{:S(2)}) collective-permute-start(bf16[512,2,416]{0,2,1:T(8,128)(2,1)} %get-tuple-element.16), channel_id=1, source_target_pairs={{0,4},{4,8},{8,12},{12,16},{16,20},{20,24},{24,28},{1,5},{5,9},{9,... | collective-permute-start | bytes 2555912 | tf_op jit(solution)/shard_map/ppermute | solution.py:19
  39.6 5.2 %collective-permute-start.2 = (bf16[512,2,416]{0,2,1:T(8,128)(2,1)}, bf16[512,2,416]{0,2,1:T(8,128)(2,1)}, u32[]{:S(2)}, u32[]{:S(2)}) collective-permute-start(bf16[512,2,416]{0,2,1:T(8,128)(2,1)} %get-tuple-element.16), channel_id=1, source_target_pairs={{0,8},{4,12},{8,16},{12,20},{16,24},{20,28},{1,9},{5,13},{9,17},{1... | collective-permute-start | bytes 2555912 | tf_op jit(solution)/shard_map/ppermute | solution.py:19
  49.9 1.8 slice.49
  51.7 2.7 compare_and_fusion
  55.3 2.2 constant_dynamic-update-slice_fusion.3
  57.5 18.4 %collective-permute-done.1 = bf16[512,2,416]{0,2,1:T(8,128)(2,1)} collective-permute-done((bf16[512,2,416]{0,2,1:T(8,128)(2,1)}, bf16[512,2,416]{0,2,1:T(8,128)(2,1)}, u32[]{:S(2)}, u32[]{:S(2)}) %collective-permute-start.1) | collective-permute-done | bytes 852000 | tf_op jit(solution)/shard_map/ppermute | solution.py:19
  75.9 2.2 constant_dynamic-update-slice_fusion.2
  78.0 2.3 constant_dynamic-update-slice_fusion.1
  80.3 2.2 constant_dynamic-update-slice_fusion
  82.5 4.6 fusion.161
  87.1 15.3 %fusion.163 = (f32[4,512]{1,0:T(4,128)S(1)}, bf16[4,512,2560]{2,1,0:T(8,128)(2,1)}) fusion(pred[512,2560]{1,0:T(8,128)(4,1)} %compare_and_fusion, bf16[512,4,104]{0,2,1:T(8,128)(2,1)} %bitcast.90, bf16[2560,4,104]{0,2,1:T(8,128)(2,1)} %bitcast.84), kind=kOutput, calls=%fused_computation.269 | convolution fusion | flops 2217740800 | bytes 14360576 | tf_op jit(solution)/shard_map/sub | solution.py:118
  102.4 8.0 %fusion.70 = bf16[512,4,104]{0,2,1:T(8,128)(2,1)S(1)} fusion(bf16[2560,4,104]{0,2,1:T(8,128)(2,1)} %bitcast.83, bf16[4,512,2560]{2,1,0:T(8,128)(2,1)} %get-tuple-element.33, f32[512,4]{0,1:T(4,128)S(1)} %maximum_bitcast_fusion), kind=kOutput, calls=%fused_computation.85 | convolution fusion | flops 1090945024 | bytes 13049856 | tf_op jit(solution)/shard_map/hqk,khe->qhe/dot_general | solution.py:120
  110.4 2.3 convolution_convert_fusion
  113.0 57.9 %all-reduce.2.cloned.1.call-done = bf16[512,1664]{1,0:T(8,128)(2,1)} async-done(((bf16[512,1664]{1,0:T(8,128)(2,1)}), bf16[512,1664]{1,0:T(8,128)(2,1)}) %all-reduce.2.cloned.1.call-update) | async-done | bytes 1703952 | tf_op jit(solution)/shard_map/psum | solution.py:137
  171.0 3.6 fusion.160
  176.8 22.0 %convolution_convert_fusion.1 = bf16[512,1664]{1,0:T(8,128)(2,1)} fusion(bf16[2048,1664]{1,0:T(8,128)(2,1)} %param.23, bf16[1664,2048]{1,0:T(8,128)(2,1)} %param.22, f32[512,1664]{1,0:T(8,128)} %copy-done.1, f32[1664]{0:T(1024)S(1)} %copy-done.13, f32[512]{0:T(512)S(1)} %add_rsqrt_fusion, f32[512]{0:T(512)S(1)} %broadcast_multiply_fusion), kind=kOutput, calls=%fused_computation.40 | convolution fusion | flops 7051739136 | bytes 18754048 | tf_op jit(solution)/shard_map/dot_general | solution.py:142
  198.8 3.0 convert_element_type.86
  203.6 5.0 %reshape.195 = f32[128,4,1664]{2,1,0:T(4,128)} reshape(f32[512,1664]{1,0:T(8,128)} %copy-done.1) | data formatting | bytes 6815744 | tf_op jit(solution)/shard_map/reshape | solution.py:133
  208.6 2.7 constant_dynamic-slice_fusion.2
  211.3 17.8 %reduce-scatter.3.cloned.1.call-done = bf16[1,128,1664]{2,1,0:T(8,128)(2,1)} async-done(((bf16[4,128,1664]{2,1,0:T(8,128)(2,1)}), bf16[1,128,1664]{2,1,0:T(8,128)(2,1)}) %reduce-scatter.3.cloned.1.call-update) | async-done | bytes 426000 | tf_op jit(solution)/shard_map/reduce_scatter | solution.py:143
  229.1 1.9 fusion.74
  231.1 65.5 %all-gather.2.cloned.1.call-done = bf16[1024,1664]{1,0:T(8,128)(2,1)} async-done(((bf16[128,1664]{1,0:T(8,128)(2,1)}), bf16[1024,1664]{1,0:T(8,128)(2,1)}) %all-gather.2.cloned.1.call-update) | async-done | bytes 3407888 | tf_op jit(solution)/shard_map/all_gather | solution.py:151
  296.6 5.0 %convolution_convert_fusion.3 = bf16[1024,512]{1,0:T(8,128)(2,1)} fusion(bf16[1024,1664]{1,0:T(8,128)(2,1)} %all-gather.2.cloned.1.call-done, bf16[1664,512]{1,0:T(8,128)(2,1)S(1)} %copy-done), kind=kOutput, calls=%fused_computation.81 | convolution fusion | flops 1745354752 | bytes 6160384 | tf_op jit(solution)/shard_map/dot_general | solution.py:154
  304.6 16.4 %reduce-scatter.5.cloned.1.call-done = bf16[256,512]{1,0:T(8,128)(2,1)} async-done(((bf16[1024,512]{1,0:T(8,128)(2,1)}), bf16[256,512]{1,0:T(8,128)(2,1)}) %reduce-scatter.5.cloned.1.call-update) | async-done | bytes 262160 | tf_op jit(solution)/shard_map/reduce_scatter | solution.py:153
  321.1 2.1 convolution_convert_fusion.4
  323.1 6.3 %all-to-all-start = ((bf16[8,64,512]{2,1,0:T(8,128)(2,1)}), bf16[8,64,512]{2,1,0:T(8,128)(2,1)S(1)}, u32[]{:S(2)}, u32[]{:S(2)}) async-start(bf16[8,64,512]{2,1,0:T(8,128)(2,1)} %bitcast.16), calls=%async_computation.2 | async-start | bytes 1048576 | tf_op jit(solution)/shard_map/all_to_all | solution.py:192
  330.8 66.3 %psum.15 = f32[4,19]{1,0:T(4,128)S(1)} all-reduce(f32[4,19]{1,0:T(4,128)S(1)} %get-tuple-element.31), channel_id=1, replica_groups=mesh['dp'=4,'seq'=8,'tensor'=4] {'dp','seq','tensor'}, use_global_device_ids=true, to_apply=%region_16.18 | all-reduce | flops 76 | bytes 608 | tf_op jit(solution)/shard_map/psum | solution.py:174
  397.1 62.6 %pmax.7 = f32[4,19]{1,0:T(4,128)S(1)} all-reduce(f32[4,19]{1,0:T(4,128)S(1)} %get-tuple-element.30), channel_id=1, replica_groups=mesh['dp'=4,'seq'=8,'tensor'=4] {'dp','seq','tensor'}, use_global_device_ids=true, to_apply=%region_19.21 | all-reduce | flops 76 | bytes 608 | tf_op jit(solution)/shard_map/pmax | solution.py:175
  (101 shorter events, 32.7 us)
Async XLA Ops:
  7.2 289.4 %copy-start = (bf16[1664,512]{1,0:T(8,128)(2,1)S(1)}, bf16[1664,512]{1,0:T(8,128)(2,1)}, u32[]{:S(2)}) copy-start(bf16[1664,512]{1,0:T(8,128)(2,1)} %param.24) | copy-start | bytes 5111812
  7.2 163.8 %all-reduce.2.cloned.1.call-start = ((), (), s32[]{:S(2)}) async-start(), calls=%async_computation.3 | async-start | bytes 3407872 | tf_op jit(solution)/shard_map/psum | solution.py:137
  14.0 1.6 copy-start.8
  21.1 2.1 copy-start.4
  21.1 2.6 copy-start.3
  23.7 2.4 copy-start.2
  23.7 2.8 copy-start.10
  23.7 2.8 copy-start.12
  29.4 1.1 copy-start.5
  31.9 23.4 %collective-permute-start = (bf16[512,2,416]{0,2,1:T(8,128)(2,1)}, bf16[512,2,416]{0,2,1:T(8,128)(2,1)}, u32[]{:S(2)}, u32[]{:S(2)}) collective-permute-start(bf16[512,2,416]{0,2,1:T(8,128)(2,1)} %get-tuple-element.16), channel_id=1, source_target_pairs={{0,4},{4,8},{8,12},{12,16},{16,20},{20,24},{24,28},{1,5},{5,9},{9,... | collective-permute-start | bytes 2555912 | tf_op jit(solution)/shard_map/ppermute | solution.py:19
  38.3 37.5 %collective-permute-start.1 = (bf16[512,2,416]{0,2,1:T(8,128)(2,1)}, bf16[512,2,416]{0,2,1:T(8,128)(2,1)}, u32[]{:S(2)}, u32[]{:S(2)}) collective-permute-start(bf16[512,2,416]{0,2,1:T(8,128)(2,1)} %get-tuple-element.16), channel_id=1, source_target_pairs={{4,0},{8,4},{12,8},{16,12},{20,16},{24,20},{28,24},{5,1},{9,5},{13... | collective-permute-start | bytes 2555912 | tf_op jit(solution)/shard_map/ppermute | solution.py:19
  39.6 38.4 %collective-permute-start.2 = (bf16[512,2,416]{0,2,1:T(8,128)(2,1)}, bf16[512,2,416]{0,2,1:T(8,128)(2,1)}, u32[]{:S(2)}, u32[]{:S(2)}) collective-permute-start(bf16[512,2,416]{0,2,1:T(8,128)(2,1)} %get-tuple-element.16), channel_id=1, source_target_pairs={{0,8},{4,12},{8,16},{12,20},{16,24},{20,28},{1,9},{5,13},{9,17},{1... | collective-permute-start | bytes 2555912 | tf_op jit(solution)/shard_map/ppermute | solution.py:19
  44.9 35.4 %collective-permute-start.3 = (bf16[512,2,416]{0,2,1:T(8,128)(2,1)}, bf16[512,2,416]{0,2,1:T(8,128)(2,1)}, u32[]{:S(2)}, u32[]{:S(2)}) collective-permute-start(bf16[512,2,416]{0,2,1:T(8,128)(2,1)} %get-tuple-element.16), channel_id=1, source_target_pairs={{8,0},{12,4},{16,8},{20,12},{24,16},{28,20},{9,1},{13,5},{17,9},{2... | collective-permute-start | bytes 2555912 | tf_op jit(solution)/shard_map/ppermute | solution.py:19
  102.4 8.0 %copy-start.11 = (bf16[416,1664]{1,0:T(8,128)(2,1)S(1)}, bf16[416,1664]{1,0:T(8,128)(2,1)}, u32[]{:S(2)}) copy-start(bf16[416,1664]{1,0:T(8,128)(2,1)} %param.20) | copy-start | bytes 4153348
  112.7 64.0 %copy-start.13 = (f32[1664]{0:T(1024)S(1)}, f32[1664]{0:T(1024)}, u32[]{:S(2)}) copy-start(f32[1664]{0:T(1024)} %param.21) | copy-start | bytes 19972
  112.7 116.4 %reduce-scatter.3.cloned.1.call-start = ((), (), s32[]{:S(2)}) async-start(), calls=%async_computation.4 | async-start | bytes 2129920 | tf_op jit(solution)/shard_map/reduce_scatter | solution.py:143
  174.6 1.7 copy-start.1
  203.2 93.4 %all-gather.2.cloned.1.call-start = ((), (), s32[]{:S(2)}) async-start(), calls=%async_computation.5 | async-start | bytes 3833856 | tf_op jit(solution)/shard_map/all_gather | solution.py:151
  231.0 70.6 %copy-start.6 = (s32[4096]{0:T(1024)S(1)}, s32[4096]{0:T(1024)}, u32[]{:S(2)}) copy-start(s32[4096]{0:T(1024)} %param.16) | copy-start | bytes 49156
  231.0 71.2 %copy-start.7 = (s32[4096]{0:T(1024)S(1)}, s32[4096]{0:T(1024)}, u32[]{:S(2)}) copy-start(s32[4096]{0:T(1024)} %param.17) | copy-start | bytes 49156
  231.0 90.0 %reduce-scatter.5.cloned.1.call-start = ((), (), s32[]{:S(2)}) async-start(), calls=%async_computation.6 | async-start | bytes 1310720 | tf_op jit(solution)/shard_map/reduce_scatter | solution.py:153
  301.6 158.6 %copy-start.9 = (s32[19,2]{0,1:T(2,128)S(1)}, s32[19,2]{0,1:T(2,128)}, u32[]{:S(2)}) copy-start(s32[19,2]{0,1:T(2,128)} %param.15) | copy-start | bytes 460
  323.1 137.7 %all-to-all-start = ((bf16[8,64,512]{2,1,0:T(8,128)(2,1)}), bf16[8,64,512]{2,1,0:T(8,128)(2,1)S(1)}, u32[]{:S(2)}, u32[]{:S(2)}) async-start(bf16[8,64,512]{2,1,0:T(8,128)(2,1)} %bitcast.16), calls=%async_computation.2 | async-start | bytes 1048576 | tf_op jit(solution)/shard_map/all_to_all | solution.py:192
Sparse Core Ops, SparseCore 0:
  112.9 58.0 all-reduce.1
  203.3 25.7 reduce-scatter.2
  232.0 64.5 all-gather.1
  301.8 19.2 reduce-scatter.4
